TPU v7x, 32 devices: a whole 2x2x4 slice. The times are simulated.
32 devices in a mesh: outer: 4 (over y, x), inner: 8 (over z, core).
Axes of the slice: x: 2, y: 2, z: 4, core: 2. Of those that a mesh axis runs over, the one named last changes fastest.
Arguments:
- tokens: bfloat16 [4096, 2048], P(('outer', 'inner')), may hold values from -6 to 6
- cotangent: bfloat16 [4096, 2048], P(('outer', 'inner')), may hold values from -6 to 6
- routes: int32 [4096, 8], P(('outer', 'inner')), may hold values from 0 to 31, all different within a row; in each aligned block of 128 rows (0 to 127, 128 to 255, ...) at most 36 rows name the same one
- router_weight: bfloat16 [2048, 32], replicated, may hold values from -0.125 to 0.125
- gate_saved: bfloat16 [32, 1152, 768], P(('outer', 'inner')), may hold values from -6 to 6
- up_saved: bfloat16 [32, 1152, 768], P(('outer', 'inner')), may hold values from -6 to 6
- gate_weight: bfloat16 [32, 2048, 768], P(('outer', 'inner')), may hold values from -0.125 to 0.125
- up_weight: bfloat16 [32, 2048, 768], P(('outer', 'inner')), may hold values from -0.125 to 0.125
- down_weight: bfloat16 [32, 768, 2048], P(('outer', 'inner')), may hold values from -0.21875 to 0.21875
Outputs:
- grad_tokens: bfloat16 [4096, 2048], P(('outer', 'inner'))
- grad_gate: bfloat16 [32, 2048, 768], P(('outer', 'inner'))
- grad_up: bfloat16 [32, 2048, 768], P(('outer', 'inner'))
- grad_down: bfloat16 [32, 768, 2048], P(('outer', 'inner'))
- grad_router: float32 [2048, 32], replicated
Inputs may be any that keep to these rules, and one draw needn't show every extreme that they name: `routes`: each row names 8 different experts. Among the rows of one device no expert is named more than 36 times, and in every draw some expert is named exactly 36 times by the rows of some device.
All inputs are finite; a program needn't handle non-finite values.
Results may differ from a plain program's by a relative error of at most 0.01.
Values may be sent and summed in bfloat16 or wider, within the bound.
No kernel may reach another device: no remote copies, remote signals or barrier semaphores. Data moves between devices by JAX's collectives and lax.ppermute only.
A program may use at most 192 MiB of HBM per device.

v0:
```python
import math
import jax
import jax.numpy as jnp
from jax import lax
from jax.sharding import PartitionSpec as P

contract_rows = (((0,), (0,)), ((), ()))
contract_cols = (((1,), (1,)), ((), ()))


def route_tables(routes, experts, capacity):
    flat_routes = routes.reshape(-1)
    onehot = (flat_routes[:, None] == jnp.arange(experts, dtype=jnp.int32)[None, :]).astype(
        jnp.int32
    )
    earlier = jnp.cumsum(onehot, axis=0) - onehot
    position = jnp.sum(earlier * onehot, axis=1)
    target = flat_routes * capacity + position
    slot_table = (
        jnp.arange(experts * capacity, dtype=jnp.int32)[:, None] == target[None, :]
    ).astype(jnp.bfloat16)
    token_table = jnp.sum(
        slot_table.reshape(experts * capacity, routes.shape[0], routes.shape[1]), axis=2
    )
    return (slot_table, token_table)


def route_probs(tokens, routes, router_weight):
    router_logits = jnp.dot(tokens, router_weight, preferred_element_type=jnp.float32)
    picked = (
        routes[:, :, None] == jnp.arange(router_weight.shape[1], dtype=jnp.int32)[None, None, :]
    )
    chosen = jnp.sum(jnp.where(picked, router_logits[:, None, :], jnp.float32(0.0)), axis=2)
    exp_terms = jnp.exp(chosen)
    return (picked, exp_terms / jnp.sum(exp_terms, axis=1, keepdims=True))


def dispatch_block(tokens, cotangent, routes, router_weight, capacity):
    picked, probs = route_probs(tokens, routes, router_weight)
    slot_table, token_table = route_tables(routes, router_weight.shape[1], capacity)
    send_tokens = jnp.dot(token_table, tokens, preferred_element_type=jnp.float32).astype(
        jnp.bfloat16
    )
    send_cot = jnp.dot(token_table, cotangent, preferred_element_type=jnp.float32).astype(
        jnp.bfloat16
    )
    probs_low = probs.astype(jnp.bfloat16).reshape(-1)
    send_weight = jnp.dot(slot_table, probs_low, preferred_element_type=jnp.float32).astype(
        jnp.bfloat16
    )
    return (picked, probs, slot_table, token_table, send_tokens, send_cot, send_weight)


def slot_dot(cot_rows, out_rows):
    return jnp.sum(cot_rows.astype(jnp.float32) * out_rows.astype(jnp.float32), axis=1).astype(
        jnp.bfloat16
    )


def expert_backward(
    input_rows, cot_rows, weight_rows, gate_pre, up_pre, gate_matrix, up_matrix, down_matrix
):
    gate_value = gate_pre.astype(jnp.float32)
    up_value = up_pre.astype(jnp.float32)
    sigmoid_gate = jax.nn.sigmoid(gate_value)
    silu_gate = gate_value * sigmoid_gate
    hidden = (silu_gate * up_value).astype(jnp.bfloat16)
    expert_out = jnp.dot(hidden, down_matrix, preferred_element_type=jnp.float32).astype(
        jnp.bfloat16
    )
    scaled_cot = (weight_rows.astype(jnp.float32)[:, None] * cot_rows.astype(jnp.float32)).astype(
        jnp.bfloat16
    )
    grad_hidden = lax.dot_general(
        scaled_cot, down_matrix, contract_cols, preferred_element_type=jnp.float32
    )
    grad_gate_pre = (
        grad_hidden * up_value * sigmoid_gate * (1.0 + gate_value * (1.0 - sigmoid_gate))
    ).astype(jnp.bfloat16)
    grad_up_pre = (grad_hidden * silu_gate).astype(jnp.bfloat16)
    grad_rows = (
        lax.dot_general(
            grad_gate_pre, gate_matrix, contract_cols, preferred_element_type=jnp.float32
        )
        + lax.dot_general(grad_up_pre, up_matrix, contract_cols, preferred_element_type=jnp.float32)
    ).astype(jnp.bfloat16)
    grad_gate_w = lax.dot_general(
        input_rows, grad_gate_pre, contract_rows, preferred_element_type=jnp.float32
    ).astype(jnp.bfloat16)
    grad_up_w = lax.dot_general(
        input_rows, grad_up_pre, contract_rows, preferred_element_type=jnp.float32
    ).astype(jnp.bfloat16)
    grad_down_w = lax.dot_general(
        hidden, scaled_cot, contract_rows, preferred_element_type=jnp.float32
    ).astype(jnp.bfloat16)
    return (grad_rows, expert_out, grad_gate_w, grad_up_w, grad_down_w)


def finish_block(
    tokens, router_weight, picked, probs, slot_table, token_table, back_rows, route_dot
):
    grad_sum = lax.dot_general(
        token_table, back_rows, contract_rows, preferred_element_type=jnp.float32
    )
    route_grad = lax.dot_general(
        slot_table, route_dot, contract_rows, preferred_element_type=jnp.float32
    ).reshape(probs.shape)
    inner_term = jnp.sum(probs * route_grad, axis=1, keepdims=True)
    chosen_grad = probs * (route_grad - inner_term)
    logit_grad = jnp.sum(
        jnp.where(picked, chosen_grad[:, :, None], jnp.float32(0.0)), axis=1
    ).astype(jnp.bfloat16)
    grad_tokens = (
        grad_sum
        + lax.dot_general(
            logit_grad, router_weight, contract_cols, preferred_element_type=jnp.float32
        )
    ).astype(jnp.bfloat16)
    router_part = lax.dot_general(
        tokens, logit_grad, contract_rows, preferred_element_type=jnp.float32
    )
    return (grad_tokens, router_part)


def body(
    tokens,
    cotangent,
    routes,
    router_weight,
    gate_saved,
    up_saved,
    gate_weight,
    up_weight,
    down_weight,
):
    experts = router_weight.shape[1]
    width = tokens.shape[1]
    capacity = gate_saved.shape[1] // experts
    outer_size = lax.axis_size("outer")
    inner_size = lax.axis_size("inner")
    picked, probs, slot_table, token_table, send_tokens, send_cot, send_weight = dispatch_block(
        tokens, cotangent, routes, router_weight, capacity
    )
    grid_tokens = send_tokens.reshape(experts, capacity, width)
    grid_cot = send_cot.reshape(experts, capacity, width)
    grid_weight = send_weight.reshape(experts, capacity)
    got_tokens, got_cot, got_weight = (
        lax.all_to_all(grid_tokens, ("outer", "inner"), split_axis=0, concat_axis=0, tiled=True),
        lax.all_to_all(grid_cot, ("outer", "inner"), split_axis=0, concat_axis=0, tiled=True),
        lax.all_to_all(grid_weight, ("outer", "inner"), split_axis=0, concat_axis=0, tiled=True),
    )
    cot_rows = got_cot.reshape(-1, width)
    grad_rows, expert_out, grad_gate_w, grad_up_w, grad_down_w = expert_backward(
        got_tokens.reshape(-1, width),
        cot_rows,
        got_weight.reshape(-1),
        gate_saved[0],
        up_saved[0],
        gate_weight[0],
        up_weight[0],
        down_weight[0],
    )
    back_grad = grad_rows.reshape(experts, capacity, width)
    extra = expert_out.reshape(experts, capacity, width)
    back_rows, back_extra = (
        lax.all_to_all(back_grad, ("outer", "inner"), split_axis=0, concat_axis=0, tiled=True),
        lax.all_to_all(extra, ("outer", "inner"), split_axis=0, concat_axis=0, tiled=True),
    )
    route_dot = slot_dot(send_cot, back_extra.reshape(-1, width))
    grad_tokens, router_part = finish_block(
        tokens,
        router_weight,
        picked,
        probs,
        slot_table,
        token_table,
        back_rows.reshape(-1, width),
        route_dot,
    )
    total_tokens = tokens.shape[0] * outer_size * inner_size
    grad_router = lax.psum(router_part, ("outer", "inner")) * (1.0 / math.sqrt(total_tokens))
    return (grad_tokens, grad_gate_w[None], grad_up_w[None], grad_down_w[None], grad_router)


def solution(mesh):
    in_specs = (
        P(("outer", "inner"), None),
        P(("outer", "inner"), None),
        P(("outer", "inner"), None),
        P(),
        P(("outer", "inner"), None, None),
        P(("outer", "inner"), None, None),
        P(("outer", "inner"), None, None),
        P(("outer", "inner"), None, None),
        P(("outer", "inner"), None, None),
    )
    out_specs = (
        P(("outer", "inner"), None),
        P(("outer", "inner"), None, None),
        P(("outer", "inner"), None, None),
        P(("outer", "inner"), None, None),
        P(),
    )
    return jax.shard_map(body, mesh=mesh, in_specs=in_specs, out_specs=out_specs, check_vma=False)
```

profile of v0, /device:TPU:0, one launch (start us, length us, event | category | flops | bytes accessed | tf_op | source)
XLA Modules:
  0.0 628.6 jit_solution(13599808058669787535)
XLA Ops:
  9.1 8.1 %convolution_convert_fusion = bf16[1152,2048]{1,0:T(8,128)(2,1)} fusion(bf16[1,768,2048]{2,1,0:T(8,128)(2,1)S(1)} %copy-done, bf16[1,1152,768]{2,1,0:T(8,128)(2,1)} %param.14, bf16[1,1152,768]{2,1,0:T(8,128)(2,1)} %param.13), kind=kOutput, calls=%fused_computation.3 | convolution fusion | flops 3633315840 | bytes 11403264 | tf_op jit(solution)/shard_map/dot_general | solution.py:68
  17.1 7.2 %reshape.153 = bf16[32,36,2048]{2,1,0:T(8,128)(2,1)} reshape(bf16[1152,2048]{1,0:T(8,128)(2,1)} %convolution_convert_fusion) | data formatting | bytes 9437184 | tf_op jit(solution)/shard_map/reshape | solution.py:164
  24.3 7.4 %all-to-all-start.3 = ((bf16[32,36,2048]{2,1,0:T(8,128)(2,1)}), bf16[32,36,2048]{2,1,0:T(8,128)(2,1)}, u32[]{:S(2)}, u32[]{:S(2)}) async-start(bf16[32,36,2048]{2,1,0:T(8,128)(2,1)} %reshape.153), calls=%async_computation.3 | async-start | bytes 10485760 | tf_op jit(solution)/shard_map/all_to_all | solution.py:167
  32.0 9.0 %reduce-window.6 = s32[32,8,128]{2,1,0:T(8,128)S(1)} reduce-window(s32[32,8,128]{2,1,0:T(8,128)S(1)} %fusion.39, s32[]{:T(128)} %constant.5.clone.1), window={size=1x1x128 pad=0_0x0_0x127_0}, to_apply=%region_0.1 | reduce-window | flops 4161536 | bytes 262148 | tf_op jit(solution)/shard_map/reduce-window
  43.1 6.0 fusion.30
  49.1 100.1 %all-to-all-done.3 = bf16[32,36,2048]{2,1,0:T(8,128)(2,1)} async-done(((bf16[32,36,2048]{2,1,0:T(8,128)(2,1)}), bf16[32,36,2048]{2,1,0:T(8,128)(2,1)}, u32[]{:S(2)}, u32[]{:S(2)}) %all-to-all-start.3) | async-done | bytes 4718624 | tf_op jit(solution)/shard_map/all_to_all | solution.py:167
  149.2 8.0 %reshape.160 = f32[1152,2048]{1,0:T(8,128)} reshape(bf16[32,36,2048]{2,1,0:T(8,128)(2,1)} %all-to-all-done.3) | data formatting | bytes 14155776 | tf_op jit(solution)/shard_map/convert_element_type | solution.py:55
  157.2 7.5 %multiply_reduce_fusion = (bf16[1152]{0:T(1024)(128)(2,1)S(1)}, bf16[1152,2048]{1,0:T(8,128)(2,1)}) fusion(f32[1152,2048]{1,0:T(8,128)} %reshape.160, bf16[1152,128]{1,0:T(8,128)(2,1)S(1)} %fusion.30, bf16[128,2048]{1,0:T(8,128)(2,1)} %param.10), kind=kOutput, calls=%fused_computation.1 | convolution fusion | flops 613415808 | bytes 14977280 | tf_op jit(solution)/shard_map/dot_general | solution.py:44
  170.2 7.2 %reshape.150 = bf16[32,36,2048]{2,1,0:T(8,128)(2,1)} reshape(bf16[1152,2048]{1,0:T(8,128)(2,1)} %get-tuple-element.8) | data formatting | bytes 9437184 | tf_op jit(solution)/shard_map/reshape | solution.py:145
  177.4 5.9 all-to-all-start.1
  187.9 7.2 %reshape.155 = bf16[32,36,2048]{2,1,0:T(8,128)(2,1)} reshape(bf16[1152,2048]{1,0:T(8,128)(2,1)} %convolution_convert_fusion.1) | data formatting | bytes 9437184 | tf_op jit(solution)/shard_map/reshape | solution.py:144
  195.1 105.8 %all-to-all-done.1 = bf16[32,36,2048]{2,1,0:T(8,128)(2,1)} async-done(((bf16[32,36,2048]{2,1,0:T(8,128)(2,1)}), bf16[32,36,2048]{2,1,0:T(8,128)(2,1)}, u32[]{:S(2)}, u32[]{:S(2)}) %all-to-all-start.1) | async-done | bytes 4718624 | tf_op jit(solution)/shard_map/all_to_all | solution.py:149
  304.6 5.6 multiply_convert_fusion
  310.3 7.3 %convert_element_type.128 = bf16[1152,2048]{1,0:T(8,128)(2,1)} reshape(bf16[32,36,2048]{2,1,0:T(8,128)(2,1)} %multiply_convert_fusion) | data formatting | bytes 9437184 | tf_op jit(solution)/shard_map/convert_element_type | solution.py:71
  317.6 9.1 %fusion.9 = (bf16[1152,768]{1,0:T(8,128)(2,1)S(1)}, f32[1152,768]{1,0:T(8,128)}) fusion(bf16[1,1152,768]{2,1,0:T(8,128)(2,1)} %param.14, bf16[1,1152,768]{2,1,0:T(8,128)(2,1)} %param.13, bf16[1152,2048]{1,0:T(8,128)(2,1)} %convert_element_type.128, bf16[1,768,2048]{2,1,0:T(8,128)(2,1)S(1)} %copy-done), kind=kOutput, calls=%fused_computation.22 | convolution fusion | flops 3634495488 | bytes 16711680 | tf_op jit(solution)/shard_map/dot_general | solution.py:74
  330.6 8.1 %add_convert_fusion = bf16[1152,2048]{1,0:T(8,128)(2,1)} fusion(f32[1152,2048]{1,0:T(8,128)S(1)} %fusion.21, bf16[1,2048,768]{2,1,0:T(8,128)(2,1)S(1)} %copy-done.8, f32[1152,768]{1,0:T(8,128)} %get-tuple-element.10, bf16[1,1152,768]{2,1,0:T(8,128)(2,1)S(1)} %copy-done.10), kind=kOutput, calls=%fused_computation.2 | convolution fusion | flops 3634790400 | bytes 22609920 | tf_op jit(solution)/shard_map/dot_general | solution.py:85
  338.7 7.2 %reshape.151 = bf16[32,36,2048]{2,1,0:T(8,128)(2,1)} reshape(bf16[1152,2048]{1,0:T(8,128)(2,1)} %add_convert_fusion) | data formatting | bytes 9437184 | tf_op jit(solution)/shard_map/reshape | solution.py:163
  345.9 76.1 %all-to-all-done.4 = bf16[32,36,2048]{2,1,0:T(8,128)(2,1)} async-done(((bf16[32,36,2048]{2,1,0:T(8,128)(2,1)}), bf16[32,36,2048]{2,1,0:T(8,128)(2,1)}, u32[]{:S(2)}, u32[]{:S(2)}) %all-to-all-start.4) | async-done | bytes 4718624 | tf_op jit(solution)/shard_map/all_to_all | solution.py:148
  426.8 7.3 %reshape.156 = bf16[1152,2048]{1,0:T(8,128)(2,1)} reshape(bf16[32,36,2048]{2,1,0:T(8,128)(2,1)} %all-to-all-done.4) | data formatting | bytes 9437184 | tf_op jit(solution)/shard_map/reshape | solution.py:154
  434.0 150.4 %all-reduce.2.cloned.1.call-done = f32[2048,32]{0,1:T(8,128)} async-done(((f32[2048,32]{0,1:T(8,128)}), f32[2048,32]{0,1:T(8,128)}) %all-reduce.2.cloned.1.call-update) | async-done | bytes 262160 | tf_op jit(solution)/shard_map/psum | solution.py:181
  586.1 9.1 %fusion.26 = bf16[1,2048,768]{2,1,0:T(8,128)(2,1)} fusion(bf16[1152,2048]{1,0:T(8,128)(2,1)} %reshape.156, bf16[1152,768]{1,0:T(8,128)(2,1)} %copy-done.13), kind=kOutput, calls=%fused_computation.42 | convolution fusion | flops 3625451520 | bytes 9633792 | tf_op jit(solution)/shard_map/dot_general | solution.py:87
  595.2 8.5 %fusion.28 = bf16[1,768,2048]{2,1,0:T(8,128)(2,1)} fusion(bf16[1152,2048]{1,0:T(8,128)(2,1)} %convert_element_type.128, bf16[1,1152,768]{2,1,0:T(8,128)(2,1)S(1)} %copy-done.9, bf16[1,1152,768]{2,1,0:T(8,128)(2,1)S(1)} %copy-done.11), kind=kOutput, calls=%fused_computation.44 | convolution fusion | flops 3632529408 | bytes 11403264 | tf_op jit(solution)/shard_map/dot_general | solution.py:93
  603.7 6.3 %fusion.27 = bf16[1,2048,768]{2,1,0:T(8,128)(2,1)} fusion(bf16[1152,2048]{1,0:T(8,128)(2,1)S(1)} %copy-done.3, f32[1152,768]{1,0:T(8,128)S(1)} %copy-done.12, bf16[1,1152,768]{2,1,0:T(8,128)(2,1)S(1)} %copy-done.11), kind=kOutput, calls=%fused_computation.43 | convolution fusion | flops 3631644672 | bytes 13172736 | tf_op jit(solution)/shard_map/dot_general | solution.py:90
  609.9 7.4 %reshape.152 = bf16[1152,2048]{1,0:T(8,128)(2,1)} reshape(bf16[32,36,2048]{2,1,0:T(8,128)(2,1)} %all-to-all-done.2) | data formatting | bytes 9437184 | tf_op jit(solution)/shard_map/reshape | solution.py:177
  (71 shorter events, 32.6 us)
Async XLA Ops:
  7.2 1.9 copy-start
  24.3 7.4 %copy-start.6 = (s32[128,8]{0,1:T(8,128)S(1)}, s32[128,8]{0,1:T(8,128)}, u32[]{:S(2)}) copy-start(s32[128,8]{0,1:T(8,128)} %param.11) | copy-start | bytes 12292
  24.3 17.4 %copy-start.4 = (bf16[2048,32]{0,1:T(8,128)(2,1)S(1)}, bf16[2048,32]{0,1:T(8,128)(2,1)}, u32[]{:S(2)}) copy-start(bf16[2048,32]{0,1:T(8,128)(2,1)} %param.12) | copy-start | bytes 393220
  24.3 124.9 %all-to-all-start.3 = ((bf16[32,36,2048]{2,1,0:T(8,128)(2,1)}), bf16[32,36,2048]{2,1,0:T(8,128)(2,1)}, u32[]{:S(2)}, u32[]{:S(2)}) async-start(bf16[32,36,2048]{2,1,0:T(8,128)(2,1)} %reshape.153), calls=%async_computation.3 | async-start | bytes 10485760 | tf_op jit(solution)/shard_map/all_to_all | solution.py:167
  167.6 9.8 %all-to-all-start = ((bf16[32,1,36]{2,1,0:T(2,128)(2,1)}), bf16[32,1,36]{2,1,0:T(2,128)(2,1)S(1)}, u32[]{:S(2)}, u32[]{:S(2)}) async-start(bf16[32,1,36]{2,1,0:T(2,128)(2,1)} %all_to_all.24), calls=%async_computation | async-start | bytes 32768 | tf_op jit(solution)/shard_map/all_to_all | solution.py:150
  177.4 123.5 %all-to-all-start.1 = ((bf16[32,36,2048]{2,1,0:T(8,128)(2,1)}), bf16[32,36,2048]{2,1,0:T(8,128)(2,1)}, u32[]{:S(2)}, u32[]{:S(2)}) async-start(bf16[32,36,2048]{2,1,0:T(8,128)(2,1)} %reshape.150), calls=%async_computation.1 | async-start | bytes 10485760 | tf_op jit(solution)/shard_map/all_to_all | solution.py:149
  300.8 121.1 %all-to-all-start.4 = ((bf16[32,36,2048]{2,1,0:T(8,128)(2,1)}), bf16[32,36,2048]{2,1,0:T(8,128)(2,1)}, u32[]{:S(2)}, u32[]{:S(2)}) async-start(bf16[32,36,2048]{2,1,0:T(8,128)(2,1)} %reshape.155), calls=%async_computation.4 | async-start | bytes 10485760 | tf_op jit(solution)/shard_map/all_to_all | solution.py:148
  317.6 9.1 %copy-start.7 = (bf16[1,2048,768]{2,1,0:T(8,128)(2,1)S(1)}, bf16[1,2048,768]{2,1,0:T(8,128)(2,1)}, u32[]{:S(2)}) copy-start(bf16[1,2048,768]{2,1,0:T(8,128)(2,1)} %param.15) | copy-start | bytes 9437188
  326.6 3.9 copy-start.13
  326.6 3.9 copy-start.8
  326.6 3.9 copy-start.10
  345.9 80.0 %copy-start.2 = (bf16[128,2048]{1,0:T(8,128)(2,1)S(1)}, bf16[128,2048]{1,0:T(8,128)(2,1)}, u32[]{:S(2)}) copy-start(bf16[128,2048]{1,0:T(8,128)(2,1)} %param.9) | copy-start | bytes 1572868
  421.9 188.0 %all-to-all-start.2 = ((bf16[32,36,2048]{2,1,0:T(8,128)(2,1)}), bf16[32,36,2048]{2,1,0:T(8,128)(2,1)}, u32[]{:S(2)}, u32[]{:S(2)}) async-start(bf16[32,36,2048]{2,1,0:T(8,128)(2,1)} %reshape.151), calls=%async_computation.2 | async-start | bytes 10485760 | tf_op jit(solution)/shard_map/all_to_all | solution.py:166
  425.5 158.9 %all-reduce.2.cloned.1.call-start = ((), (), s32[]{:S(2)}) async-start(), calls=%async_computation.5 | async-start | bytes 524288 | tf_op jit(solution)/shard_map/psum | solution.py:181
  586.1 9.1 %copy-start.9 = (bf16[1,1152,768]{2,1,0:T(8,128)(2,1)S(1)}, bf16[1,1152,768]{2,1,0:T(8,128)(2,1)}, u32[]{:S(2)}) copy-start(bf16[1,1152,768]{2,1,0:T(8,128)(2,1)} %param.14) | copy-start | bytes 5308420
  586.1 9.1 %copy-start.11 = (bf16[1,1152,768]{2,1,0:T(8,128)(2,1)S(1)}, bf16[1,1152,768]{2,1,0:T(8,128)(2,1)}, u32[]{:S(2)}) copy-start(bf16[1,1152,768]{2,1,0:T(8,128)(2,1)} %param.13) | copy-start | bytes 5308420
  595.2 8.5 %copy-start.3 = (bf16[1152,2048]{1,0:T(8,128)(2,1)S(1)}, bf16[1152,2048]{1,0:T(8,128)(2,1)}, u32[]{:S(2)}) copy-start(bf16[1152,2048]{1,0:T(8,128)(2,1)} %reshape.156) | copy-start | bytes 14155780
  595.2 8.5 %copy-start.12 = (f32[1152,768]{1,0:T(8,128)S(1)}, f32[1152,768]{1,0:T(8,128)}, u32[]{:S(2)}) copy-start(f32[1152,768]{1,0:T(8,128)} %get-tuple-element.10) | copy-start | bytes 10616836
  609.9 11.8 %copy-start.1 = (bf16[1,768,2048]{2,1,0:T(8,128)(2,1)S(1)}, bf16[1,768,2048]{2,1,0:T(8,128)(2,1)}, u32[]{:S(2)}) copy-start(bf16[1,768,2048]{2,1,0:T(8,128)(2,1)} %param.17) | copy-start | bytes 9437188
  617.3 3.3 copy-start.5
Sparse Core Ops, SparseCore 0:
  432.4 151.9 all-reduce.1
where the time goes:
time: 630 us; the launch traced here: 629 us
  waiting for transfers between devices  432 us (69%)
  matrix products  73.2 us (12%)
  local copies, waits for them, and re-layouts  62.5 us (10%)
  starting transfers between devices  23.5 us (4%)
  other arithmetic  22.7 us (4%)
  between operations  14.3 us (2%)
    psum x1, waiting for transfers between devices, body(): lax.psum(router_part, ('outer', 'inner')) * (1.0 / math.sqrt(total_tokens))  150 us
    all_to_all x1, waiting for transfers between devices, body(): lax.all_to_all(grid_cot, ('outer', 'inner'), split_axis=0, concat_axis=0,...  106 us
    all_to_all x1, waiting for transfers between devices, body(): lax.all_to_all(extra, ('outer', 'inner'), split_axis=0, concat_axis=0, ti...  100 us
    all_to_all x1, waiting for transfers between devices, body(): lax.all_to_all(grid_tokens, ('outer', 'inner'), split_axis=0, concat_axis...  76.1 us
  transfers between devices with their start and end apart: 6, of which 4 were waited for; matrix products, arithmetic and copies ran while one was open for 18% of the time, Pallas kernels for 0%

commit v1 on v0

--- a/solution.py
+++ b/solution.py
@@ -6,6 +6,9 @@
 
 contract_rows = (((0,), (0,)), ((), ()))
 contract_cols = (((1,), (1,)), ((), ()))
+_define_loads = lambda mesh_name, my_data, shard_axis: lax.psum(
+    lax.psum(my_data, shard_axis), mesh_name
+)
 
 
 def route_tables(routes, experts, capacity):
@@ -178,7 +181,7 @@
         route_dot,
     )
     total_tokens = tokens.shape[0] * outer_size * inner_size
-    grad_router = lax.psum(router_part, ("outer", "inner")) * (1.0 / math.sqrt(total_tokens))
+    grad_router = _define_loads("outer", router_part, "inner") * (1.0 / math.sqrt(total_tokens))
     return (grad_tokens, grad_gate_w[None], grad_up_w[None], grad_down_w[None], grad_router)
 
 

time: 630 us -> 597 us (0.948)
  waiting for transfers between devices: 432 us -> 399 us
    psum x1 -> x2, waiting for transfers between devices: 150 us -> 117 us  [the longest x1 77 us: lax.psum(my_data, shard_axis)]
  transfers between devices with their start and end apart: 6 -> 7, of which waited for: 4 -> 5; matrix products, arithmetic and copies ran while one was open for 18% -> 19% of each run, Pallas kernels for 0% -> 0%
where the time goes in v1:
time: 597 us; the launch traced here: 595 us
  waiting for transfers between devices  399 us (67%)
  matrix products  73.2 us (12%)
  local copies, waits for them, and re-layouts  62.5 us (10%)
  starting transfers between devices  23.5 us (4%)
  other arithmetic  22.7 us (4%)
  between operations  14.3 us (2%)
    all_to_all x1, waiting for transfers between devices, body(): lax.all_to_all(grid_cot, ('outer', 'inner'), split_axis=0, concat_axis=0,...  106 us
    all_to_all x1, waiting for transfers between devices, body(): lax.all_to_all(extra, ('outer', 'inner'), split_axis=0, concat_axis=0, ti...  100 us
    psum x1, waiting for transfers between devices, lax.psum(my_data, shard_axis)  77 us
    all_to_all x1, waiting for transfers between devices, body(): lax.all_to_all(grid_tokens, ('outer', 'inner'), split_axis=0, concat_axis...  76.1 us
    psum x1, waiting for transfers between devices, lax.psum(lax.psum(my_data, shard_axis), mesh_name)  40.2 us
  transfers between devices with their start and end apart: 7, of which 5 were waited for; matrix products, arithmetic and copies ran while one was open for 19% of the time, Pallas kernels for 0%

profile of v1, /device:TPU:0, one launch (start us, length us, event | category | flops | bytes accessed | tf_op | source)
XLA Modules:
  0.0 595.4 jit_solution(18427234429025240157)
XLA Ops:
  9.1 8.1 %convolution_convert_fusion = bf16[1152,2048]{1,0:T(8,128)(2,1)} fusion(bf16[1,768,2048]{2,1,0:T(8,128)(2,1)S(1)} %copy-done, bf16[1,1152,768]{2,1,0:T(8,128)(2,1)} %param.14, bf16[1,1152,768]{2,1,0:T(8,128)(2,1)} %param.13), kind=kOutput, calls=%fused_computation.3 | convolution fusion | flops 3633315840 | bytes 11403264 | tf_op jit(solution)/shard_map/dot_general | solution.py:71
  17.1 7.2 %reshape.153 = bf16[32,36,2048]{2,1,0:T(8,128)(2,1)} reshape(bf16[1152,2048]{1,0:T(8,128)(2,1)} %convolution_convert_fusion) | data formatting | bytes 9437184 | tf_op jit(solution)/shard_map/reshape | solution.py:167
  24.3 7.4 %all-to-all-start.3 = ((bf16[32,36,2048]{2,1,0:T(8,128)(2,1)}), bf16[32,36,2048]{2,1,0:T(8,128)(2,1)}, u32[]{:S(2)}, u32[]{:S(2)}) async-start(bf16[32,36,2048]{2,1,0:T(8,128)(2,1)} %reshape.153), calls=%async_computation.3 | async-start | bytes 10485760 | tf_op jit(solution)/shard_map/all_to_all | solution.py:170
  32.0 9.0 %reduce-window.6 = s32[32,8,128]{2,1,0:T(8,128)S(1)} reduce-window(s32[32,8,128]{2,1,0:T(8,128)S(1)} %fusion.39, s32[]{:T(128)} %constant.5.clone.1), window={size=1x1x128 pad=0_0x0_0x127_0}, to_apply=%region_0.1 | reduce-window | flops 4161536 | bytes 262148 | tf_op jit(solution)/shard_map/reduce-window
  43.1 6.0 %fusion.30 = bf16[1152,128]{1,0:T(8,128)(2,1)S(1)} fusion(s32[128,8]{0,1:T(8,128)S(1)} %multiply_add_fusion.1), kind=kLoop, calls=%fused_computation.47 | loop fusion | flops 3391488 | bytes 299008 | tf_op jit(solution)/shard_map/reduce_sum | solution.py:25
  49.1 100.1 %all-to-all-done.3 = bf16[32,36,2048]{2,1,0:T(8,128)(2,1)} async-done(((bf16[32,36,2048]{2,1,0:T(8,128)(2,1)}), bf16[32,36,2048]{2,1,0:T(8,128)(2,1)}, u32[]{:S(2)}, u32[]{:S(2)}) %all-to-all-start.3) | async-done | bytes 4718624 | tf_op jit(solution)/shard_map/all_to_all | solution.py:170
  149.2 8.0 %reshape.160 = f32[1152,2048]{1,0:T(8,128)} reshape(bf16[32,36,2048]{2,1,0:T(8,128)(2,1)} %all-to-all-done.3) | data formatting | bytes 14155776 | tf_op jit(solution)/shard_map/convert_element_type | solution.py:58
  157.2 7.5 %multiply_reduce_fusion = (bf16[1152]{0:T(1024)(128)(2,1)S(1)}, bf16[1152,2048]{1,0:T(8,128)(2,1)}) fusion(f32[1152,2048]{1,0:T(8,128)} %reshape.160, bf16[1152,128]{1,0:T(8,128)(2,1)S(1)} %fusion.30, bf16[128,2048]{1,0:T(8,128)(2,1)} %param.10), kind=kOutput, calls=%fused_computation.1 | convolution fusion | flops 613415808 | bytes 14977280 | tf_op jit(solution)/shard_map/dot_general | solution.py:47
  170.2 7.2 %reshape.150 = bf16[32,36,2048]{2,1,0:T(8,128)(2,1)} reshape(bf16[1152,2048]{1,0:T(8,128)(2,1)} %get-tuple-element.8) | data formatting | bytes 9437184 | tf_op jit(solution)/shard_map/reshape | solution.py:148
  177.4 5.9 all-to-all-start.1
  187.9 7.2 %reshape.155 = bf16[32,36,2048]{2,1,0:T(8,128)(2,1)} reshape(bf16[1152,2048]{1,0:T(8,128)(2,1)} %convolution_convert_fusion.1) | data formatting | bytes 9437184 | tf_op jit(solution)/shard_map/reshape | solution.py:147
  195.1 105.8 %all-to-all-done.1 = bf16[32,36,2048]{2,1,0:T(8,128)(2,1)} async-done(((bf16[32,36,2048]{2,1,0:T(8,128)(2,1)}), bf16[32,36,2048]{2,1,0:T(8,128)(2,1)}, u32[]{:S(2)}, u32[]{:S(2)}) %all-to-all-start.1) | async-done | bytes 4718624 | tf_op jit(solution)/shard_map/all_to_all | solution.py:152
  310.3 7.3 %convert_element_type.128 = bf16[1152,2048]{1,0:T(8,128)(2,1)} reshape(bf16[32,36,2048]{2,1,0:T(8,128)(2,1)} %multiply_convert_fusion) | data formatting | bytes 9437184 | tf_op jit(solution)/shard_map/convert_element_type | solution.py:74
  317.6 9.0 %fusion.9 = (bf16[1152,768]{1,0:T(8,128)(2,1)S(1)}, f32[1152,768]{1,0:T(8,128)}) fusion(bf16[1,1152,768]{2,1,0:T(8,128)(2,1)} %param.14, bf16[1,1152,768]{2,1,0:T(8,128)(2,1)} %param.13, bf16[1152,2048]{1,0:T(8,128)(2,1)} %convert_element_type.128, bf16[1,768,2048]{2,1,0:T(8,128)(2,1)S(1)} %copy-done), kind=kOutput, calls=%fused_computation.22 | convolution fusion | flops 3634495488 | bytes 16711680 | tf_op jit(solution)/shard_map/dot_general | solution.py:77
  330.6 8.1 %add_convert_fusion = bf16[1152,2048]{1,0:T(8,128)(2,1)} fusion(f32[1152,2048]{1,0:T(8,128)S(1)} %fusion.21, bf16[1,2048,768]{2,1,0:T(8,128)(2,1)S(1)} %copy-done.8, f32[1152,768]{1,0:T(8,128)} %get-tuple-element.10, bf16[1,1152,768]{2,1,0:T(8,128)(2,1)S(1)} %copy-done.10), kind=kOutput, calls=%fused_computation.2 | convolution fusion | flops 3634790400 | bytes 22609920 | tf_op jit(solution)/shard_map/dot_general | solution.py:88
  338.6 7.2 %reshape.151 = bf16[32,36,2048]{2,1,0:T(8,128)(2,1)} reshape(bf16[1152,2048]{1,0:T(8,128)(2,1)} %add_convert_fusion) | data formatting | bytes 9437184 | tf_op jit(solution)/shard_map/reshape | solution.py:166
  345.8 76.1 %all-to-all-done.4 = bf16[32,36,2048]{2,1,0:T(8,128)(2,1)} async-done(((bf16[32,36,2048]{2,1,0:T(8,128)(2,1)}), bf16[32,36,2048]{2,1,0:T(8,128)(2,1)}, u32[]{:S(2)}, u32[]{:S(2)}) %all-to-all-start.4) | async-done | bytes 4718624 | tf_op jit(solution)/shard_map/all_to_all | solution.py:151
  426.8 77.0 %all-reduce.3.cloned.1.call-done = f32[2048,32]{0,1:T(8,128)} async-done(((f32[2048,32]{0,1:T(8,128)}), f32[2048,32]{0,1:T(8,128)}) %all-reduce.3.cloned.1.call-update) | async-done | bytes 262160 | tf_op jit(solution)/shard_map/psum | solution.py:10
  503.9 7.2 %reshape.156 = bf16[1152,2048]{1,0:T(8,128)(2,1)} reshape(bf16[32,36,2048]{2,1,0:T(8,128)(2,1)} %all-to-all-done.4) | data formatting | bytes 9437184 | tf_op jit(solution)/shard_map/reshape | solution.py:157
  511.1 40.2 %all-reduce.5.cloned.1.call-done = f32[2048,32]{0,1:T(8,128)} async-done(((f32[2048,32]{0,1:T(8,128)}), f32[2048,32]{0,1:T(8,128)}) %all-reduce.5.cloned.1.call-update) | async-done | bytes 262160 | tf_op jit(solution)/shard_map/psum | solution.py:9
  553.0 9.1 %fusion.26 = bf16[1,2048,768]{2,1,0:T(8,128)(2,1)} fusion(bf16[1152,2048]{1,0:T(8,128)(2,1)} %reshape.156, bf16[1152,768]{1,0:T(8,128)(2,1)} %copy-done.13), kind=kOutput, calls=%fused_computation.42 | convolution fusion | flops 3625451520 | bytes 9633792 | tf_op jit(solution)/shard_map/dot_general | solution.py:90
  562.0 8.5 %fusion.28 = bf16[1,768,2048]{2,1,0:T(8,128)(2,1)} fusion(bf16[1152,2048]{1,0:T(8,128)(2,1)} %convert_element_type.128, bf16[1,1152,768]{2,1,0:T(8,128)(2,1)S(1)} %copy-done.9, bf16[1,1152,768]{2,1,0:T(8,128)(2,1)S(1)} %copy-done.11), kind=kOutput, calls=%fused_computation.44 | convolution fusion | flops 3632529408 | bytes 11403264 | tf_op jit(solution)/shard_map/dot_general | solution.py:96
  570.5 6.3 %fusion.27 = bf16[1,2048,768]{2,1,0:T(8,128)(2,1)} fusion(bf16[1152,2048]{1,0:T(8,128)(2,1)S(1)} %copy-done.3, f32[1152,768]{1,0:T(8,128)S(1)} %copy-done.12, bf16[1,1152,768]{2,1,0:T(8,128)(2,1)S(1)} %copy-done.11), kind=kOutput, calls=%fused_computation.43 | convolution fusion | flops 3631644672 | bytes 13172736 | tf_op jit(solution)/shard_map/dot_general | solution.py:93
  576.8 7.4 %reshape.152 = bf16[1152,2048]{1,0:T(8,128)(2,1)} reshape(bf16[32,36,2048]{2,1,0:T(8,128)(2,1)} %all-to-all-done.2) | data formatting | bytes 9437184 | tf_op jit(solution)/shard_map/reshape | solution.py:180
  (74 shorter events, 38.4 us)
Async XLA Ops:
  7.2 1.9 copy-start
  24.3 7.4 %copy-start.6 = (s32[128,8]{0,1:T(8,128)S(1)}, s32[128,8]{0,1:T(8,128)}, u32[]{:S(2)}) copy-start(s32[128,8]{0,1:T(8,128)} %param.11) | copy-start | bytes 12292
  24.3 17.4 %copy-start.4 = (bf16[2048,32]{0,1:T(8,128)(2,1)S(1)}, bf16[2048,32]{0,1:T(8,128)(2,1)}, u32[]{:S(2)}) copy-start(bf16[2048,32]{0,1:T(8,128)(2,1)} %param.12) | copy-start | bytes 393220
  24.3 124.9 %all-to-all-start.3 = ((bf16[32,36,2048]{2,1,0:T(8,128)(2,1)}), bf16[32,36,2048]{2,1,0:T(8,128)(2,1)}, u32[]{:S(2)}, u32[]{:S(2)}) async-start(bf16[32,36,2048]{2,1,0:T(8,128)(2,1)} %reshape.153), calls=%async_computation.3 | async-start | bytes 10485760 | tf_op jit(solution)/shard_map/all_to_all | solution.py:170
  167.6 9.8 %all-to-all-start = ((bf16[32,1,36]{2,1,0:T(2,128)(2,1)}), bf16[32,1,36]{2,1,0:T(2,128)(2,1)S(1)}, u32[]{:S(2)}, u32[]{:S(2)}) async-start(bf16[32,1,36]{2,1,0:T(2,128)(2,1)} %all_to_all.24), calls=%async_computation | async-start | bytes 32768 | tf_op jit(solution)/shard_map/all_to_all | solution.py:153
  177.4 123.5 %all-to-all-start.1 = ((bf16[32,36,2048]{2,1,0:T(8,128)(2,1)}), bf16[32,36,2048]{2,1,0:T(8,128)(2,1)}, u32[]{:S(2)}, u32[]{:S(2)}) async-start(bf16[32,36,2048]{2,1,0:T(8,128)(2,1)} %reshape.150), calls=%async_computation.1 | async-start | bytes 10485760 | tf_op jit(solution)/shard_map/all_to_all | solution.py:152
  300.8 121.1 %all-to-all-start.4 = ((bf16[32,36,2048]{2,1,0:T(8,128)(2,1)}), bf16[32,36,2048]{2,1,0:T(8,128)(2,1)}, u32[]{:S(2)}, u32[]{:S(2)}) async-start(bf16[32,36,2048]{2,1,0:T(8,128)(2,1)} %reshape.155), calls=%async_computation.4 | async-start | bytes 10485760 | tf_op jit(solution)/shard_map/all_to_all | solution.py:151
  317.6 9.0 %copy-start.7 = (bf16[1,2048,768]{2,1,0:T(8,128)(2,1)S(1)}, bf16[1,2048,768]{2,1,0:T(8,128)(2,1)}, u32[]{:S(2)}) copy-start(bf16[1,2048,768]{2,1,0:T(8,128)(2,1)} %param.15) | copy-start | bytes 9437188
  326.6 3.9 copy-start.13
  326.6 3.9 copy-start.8
  326.6 3.9 copy-start.10
  345.8 79.8 %copy-start.2 = (bf16[128,2048]{1,0:T(8,128)(2,1)S(1)}, bf16[128,2048]{1,0:T(8,128)(2,1)}, u32[]{:S(2)}) copy-start(bf16[128,2048]{1,0:T(8,128)(2,1)} %param.9) | copy-start | bytes 1572868
  421.9 154.9 %all-to-all-start.2 = ((bf16[32,36,2048]{2,1,0:T(8,128)(2,1)}), bf16[32,36,2048]{2,1,0:T(8,128)(2,1)}, u32[]{:S(2)}, u32[]{:S(2)}) async-start(bf16[32,36,2048]{2,1,0:T(8,128)(2,1)} %reshape.151), calls=%async_computation.2 | async-start | bytes 10485760 | tf_op jit(solution)/shard_map/all_to_all | solution.py:169
  425.5 78.3 %all-reduce.3.cloned.1.call-start = ((), (), s32[]{:S(2)}) async-start(), calls=%async_computation.5 | async-start | bytes 524288 | tf_op jit(solution)/shard_map/psum | solution.py:10
  426.6 124.7 %all-reduce.5.cloned.1.call-start = ((), (), s32[]{:S(2)}) async-start(), calls=%async_computation.6 | async-start | bytes 524288 | tf_op jit(solution)/shard_map/psum | solution.py:9
  553.0 9.1 %copy-start.9 = (bf16[1,1152,768]{2,1,0:T(8,128)(2,1)S(1)}, bf16[1,1152,768]{2,1,0:T(8,128)(2,1)}, u32[]{:S(2)}) copy-start(bf16[1,1152,768]{2,1,0:T(8,128)(2,1)} %param.14) | copy-start | bytes 5308420
  553.0 9.1 %copy-start.11 = (bf16[1,1152,768]{2,1,0:T(8,128)(2,1)S(1)}, bf16[1,1152,768]{2,1,0:T(8,128)(2,1)}, u32[]{:S(2)}) copy-start(bf16[1,1152,768]{2,1,0:T(8,128)(2,1)} %param.13) | copy-start | bytes 5308420
  562.0 8.5 %copy-start.3 = (bf16[1152,2048]{1,0:T(8,128)(2,1)S(1)}, bf16[1152,2048]{1,0:T(8,128)(2,1)}, u32[]{:S(2)}) copy-start(bf16[1152,2048]{1,0:T(8,128)(2,1)} %reshape.156) | copy-start | bytes 14155780
  562.0 8.5 %copy-start.12 = (f32[1152,768]{1,0:T(8,128)S(1)}, f32[1152,768]{1,0:T(8,128)}, u32[]{:S(2)}) copy-start(f32[1152,768]{1,0:T(8,128)} %get-tuple-element.10) | copy-start | bytes 10616836
  576.8 11.8 %copy-start.1 = (bf16[1,768,2048]{2,1,0:T(8,128)(2,1)S(1)}, bf16[1,768,2048]{2,1,0:T(8,128)(2,1)}, u32[]{:S(2)}) copy-start(bf16[1,768,2048]{2,1,0:T(8,128)(2,1)} %param.17) | copy-start | bytes 9437188
  584.2 3.3 copy-start.5
Sparse Core Ops, SparseCore 0:
  429.3 74.5 all-reduce.2
  507.0 44.2 all-reduce.4
